TPU v7x, 256 devices: a whole 4x4x8 slice. The times are simulated.
256 devices in a mesh: dp: 32 (over x, z), mp: 8 (over y, core).
Axes of the slice: x: 4, y: 4, z: 8, core: 2. Of those that a mesh axis runs over, the one named last changes fastest.
Arguments:
- tokens: bfloat16 [8192, 8192], P(('dp', 'mp')), may hold values from -6 to 6
- upstream: bfloat16 [8192, 2, 28672], P(('dp', 'mp')), may hold values from -0.0625 to 0.0625
- deltas: bfloat16 [1024, 128, 128], P('mp'), may hold values from -0.5 to 0.5
- block_row: int32 [1024], P('mp'), may hold values from 0 to 63, as said below
- block_column: int32 [1024], P('mp'), may hold values from 0 to 55, as said below
- block_owner: int32 [1024], P('mp'), may hold values from 0 to 31, as said below
- block_count: int32 [8], P('mp'), may hold values from 64 to 128, as said below
Outputs:
- branch_out: bfloat16 [8192, 2, 28672], P('dp', None, 'mp')
- block_grads: float32 [8, 192, 128, 128], P('mp', 'dp')
Inputs may be any that keep to these rules, and one draw needn't show every extreme that they name: `block_row`: row tile of each slot's delta tile. `block_column`: column tile within the shard's gate columns (below 28) followed by its up columns; the tiles of one shard's slots are distinct. `block_owner`: among the live slots of one shard no dp index owns more than 6 tiles, and in every shard one dp index owns exactly 6. The live slots of a shard are its first block_count slots; some shard has all 128 live.
All inputs are finite; a program needn't handle non-finite values.
Results may differ from a plain program's by a relative error of at most 0.001.
Values may be sent and summed in bfloat16 or wider, within the bound.
No kernel may reach another device: no remote copies, remote signals or barrier semaphores. Data moves between devices by JAX's collectives and lax.ppermute only.
A program may use at most 128 MiB of HBM per device.

v0:
```python
import jax
import jax.numpy as jnp
from jax import lax
from jax.sharding import PartitionSpec as P


def pick_tiles(source, chosen):
    slot_ids = jnp.arange(chosen.shape[1], dtype=jnp.int32)
    source_index = jnp.sum(jnp.where(chosen, slot_ids[None, :], 0), axis=1)
    present = jnp.any(chosen, axis=1).astype(jnp.float32)
    return jnp.take(source, source_index, axis=0) * present[:, None, None]


def local(tokens, upstream, deltas, block_row, block_column, block_owner, block_count):
    model_width = tokens.shape[1]
    tile_size = deltas.shape[1]
    slot_count = deltas.shape[0]
    hidden = lax.all_to_all(upstream, "mp", split_axis=2, concat_axis=0, tiled=True)
    group_rows = hidden.shape[0]
    column_blocks = hidden.shape[1] * hidden.shape[2] // tile_size
    hidden_major = jnp.transpose(hidden.reshape(group_rows, column_blocks, tile_size), (1, 0, 2))
    upstream_chosen = jnp.take(hidden_major, block_column, axis=0)
    slot_ids = jnp.arange(slot_count, dtype=jnp.int32)
    live_slots = slot_ids < block_count[0]
    column_table = (
        live_slots[:, None]
        & (block_column[:, None] == jnp.arange(column_blocks, dtype=jnp.int32)[None, :])
    ).astype(jnp.float32)
    shard_rows = lax.all_gather(tokens, "mp", axis=0, tiled=True)
    row_count = shard_rows.shape[0]
    row_major = jnp.transpose(
        shard_rows.reshape(row_count, model_width // tile_size, tile_size), (1, 0, 2)
    )
    feature_tiles = jnp.take(row_major, block_row, axis=0)
    product = jnp.einsum("kni,kio->kno", feature_tiles, deltas, preferred_element_type=jnp.float32)
    rows_out = jnp.einsum("kc,kno->cno", column_table, product, precision=lax.Precision.HIGHEST)
    placed = rows_out
    grad_sum = jnp.einsum(
        "kni,kno->kio", feature_tiles, upstream_chosen, preferred_element_type=jnp.float32
    )
    placed, grad_sum = (placed, grad_sum)
    branch_out = jnp.transpose(placed.astype(jnp.bfloat16), (1, 0, 2)).reshape(
        group_rows, hidden.shape[1], hidden.shape[2]
    )
    dp_count = lax.axis_size("dp")
    owner_cap = 3 * slot_count // (2 * dp_count)
    owner_hot = (
        (block_owner[:, None] == jnp.arange(dp_count, dtype=jnp.int32)[None, :])
        & live_slots[:, None]
    ).astype(jnp.int32)
    before = jnp.cumsum(owner_hot, axis=0) - owner_hot
    owner_rank = jnp.sum(before * owner_hot, axis=1)
    summed = lax.psum(grad_sum, "dp")
    my_owner = lax.axis_index("dp")
    chosen = (
        live_slots[None, :]
        & (block_owner[None, :] == my_owner)
        & (owner_rank[None, :] == jnp.arange(owner_cap, dtype=jnp.int32)[:, None])
    )
    owned = pick_tiles(summed, chosen)
    return (branch_out, owned[None])


def solution(mesh):
    placed = (
        P(("dp", "mp"), None),
        P(("dp", "mp"), None, None),
        P("mp", None, None),
        P("mp"),
        P("mp"),
        P("mp"),
        P("mp"),
    )
    return jax.shard_map(
        local,
        mesh=mesh,
        in_specs=placed,
        out_specs=(P("dp", None, "mp"), P("mp", "dp", None, None)),
        check_vma=False,
    )
```

profile of v0, /device:TPU:6, one launch (start us, length us, event | category | flops | bytes accessed | tf_op | source)
XLA Modules:
  0.0 435.1 jit_solution(1149873122995598057)
XLA Ops:
  7.2 0.7 all-gather.2.cloned.1.call-update
  7.9 35.0 %copy.36 = bf16[32,2,28672]{0,1,2:T(2,128)(2,1)} copy(bf16[32,2,28672]{2,1,0:T(2,128)(2,1)} %param.8) | data formatting | bytes 7340032 | tf_op args[1]
  42.9 16.5 %reshape.95 = bf16[8,2,114688]{2,1,0:T(2,128)(2,1)} reshape(bf16[28672,2,32]{2,1,0:T(2,128)(2,1)} %bitcast.26) | data formatting | bytes 7340032
  59.4 4.5 %all-to-all-start = ((bf16[8,2,114688]{2,1,0:T(2,128)(2,1)}), bf16[8,2,114688]{2,1,0:T(2,128)(2,1)}, u32[]{:S(2)}, u32[]{:S(2)}) async-start(bf16[8,2,114688]{2,1,0:T(2,128)(2,1)} %reshape.95), calls=%async_computation | async-start | bytes 7340032 | tf_op jit(solution)/shard_map/all_to_all | solution.py:18
  64.0 43.9 %all-to-all-done = bf16[8,2,114688]{2,1,0:T(2,128)(2,1)} async-done(((bf16[8,2,114688]{2,1,0:T(2,128)(2,1)}), bf16[8,2,114688]{2,1,0:T(2,128)(2,1)}, u32[]{:S(2)}, u32[]{:S(2)}) %all-to-all-start) | async-done | bytes 3670048 | tf_op jit(solution)/shard_map/all_to_all | solution.py:18
  108.0 11.6 %reshape.96 = bf16[28672,2,32]{2,1,0:T(2,128)(2,1)} reshape(bf16[8,2,114688]{2,1,0:T(2,128)(2,1)} %all-to-all-done) | data formatting | bytes 7340032
  119.6 35.0 %copy.37 = bf16[32,2,8,3584]{3,1,0,2:T(2,128)(2,1)} copy(bf16[32,2,8,3584]{0,1,3,2:T(2,128)(2,1)} %bitcast.25) | data formatting | bytes 7340032 | tf_op jit(solution)/shard_map/all_to_all | solution.py:18
  154.6 9.2 %reshape.67 = bf16[256,56,128]{2,1,0:T(8,128)(2,1)} reshape(bf16[8,32,2,3584]{3,2,1,0:T(2,128)(2,1)} %bitcast.30) | data formatting | bytes 7340032 | tf_op jit(solution)/shard_map/reshape | solution.py:21
  163.8 4.8 %copy.46 = bf16[256,56,128]{2,0,1:T(8,128)(2,1)} copy(bf16[256,56,128]{2,1,0:T(8,128)(2,1)} %reshape.67) | data formatting | bytes 7340032 | tf_op jit(solution)/shard_map/reshape | solution.py:21
  168.6 8.6 %gather_fusion.1 = bf16[128,256,128]{2,1,0:T(8,128)(2,1)} fusion(bf16[56,256,128]{2,1,0:T(8,128)(2,1)} %bitcast.27, s32[1024]{0:T(1024)S(1)} %pad_clamp_fusion.1), kind=kCustom, calls=%fused_computation.1 | custom fusion | bytes 16777728 | tf_op jit(solution)/shard_map/jit(_take)/gather | solution.py:22
  177.2 6.4 %copy.33 = bf16[256,8192]{0,1:T(8,128)(2,1)} copy(bf16[256,8192]{1,0:T(8,128)(2,1)} %all-gather.2.cloned.1.call-done) | data formatting | bytes 8388608 | tf_op jit(solution)/shard_map/all_gather | solution.py:29
  183.5 6.4 %copy.34 = bf16[256,64,128]{2,0,1:T(8,128)(2,1)} copy(bf16[256,64,128]{0,2,1:T(8,128)(2,1)} %bitcast.29) | data formatting | bytes 8388608 | tf_op jit(solution)/shard_map/reshape | solution.py:32
  189.9 8.7 %gather_fusion = bf16[128,256,128]{2,1,0:T(8,128)(2,1)} fusion(bf16[64,256,128]{2,1,0:T(8,128)(2,1)} %bitcast.28, s32[1024]{0:T(1024)S(1)} %pad_clamp_fusion.2), kind=kCustom, calls=%fused_computation | custom fusion | bytes 16777728 | tf_op jit(solution)/shard_map/jit(_take)/gather | solution.py:34
  198.7 11.9 %fusion.2 = f32[128,128,128]{2,1,0:T(8,128)} fusion(bf16[128,256,128]{2,1,0:T(8,128)(2,1)} %gather_fusion.1, pred[128]{0:T(512)(128)(4,1)S(1)} %get-tuple-element.4, bf16[128,256,128]{2,1,0:T(8,128)(2,1)} %gather_fusion, pred[128]{0:T(512)(128)(4,1)S(1)} %get-tuple-element.5), kind=kOutput, calls=%fused_computation.5 | convolution fusion | flops 1082130432 | bytes 25166080 | tf_op jit(solution)/shard_map/kni,kno->kio/dot_general | solution.py:38
  211.4 0.2 reduce_window_sum.11
  211.6 0.2 select_reduce_fusion
  211.8 0.1 fusion.18
  211.9 0.1 select_reduce_fusion.1
  212.0 13.6 %fusion.6 = f32[128,256,128]{2,1,0:T(8,128)} fusion(bf16[128,128,128]{2,1,0:T(8,128)(2,1)} %param.9, bf16[128,256,128]{2,1,0:T(8,128)(2,1)} %gather_fusion, pred[128]{0:T(512)(128)(4,1)S(1)} %get-tuple-element.5), kind=kOutput, calls=%fused_computation.12 | convolution fusion | flops 1077936128 | bytes 29360256 | tf_op jit(solution)/shard_map/kni,kio->kno/dot_general | solution.py:35
  225.6 22.5 %convert_bitcast_fusion = bf16[256,56,128]{2,1,0:T(8,128)(2,1)} fusion(f32[128,256,128]{2,1,0:T(8,128)} %fusion.6, s32[128]{0:T(128)S(1)} %copy-done.1, pred[128]{0:T(512)(128)(4,1)S(1)} %get-tuple-element.3), kind=kOutput, calls=%fused_computation.11 | convolution fusion | flops 2820421632 | bytes 20447872 | tf_op jit(solution)/shard_map/kc,kno->cno/dot_general | solution.py:36
  248.1 8.2 %reshape.66 = bf16[256,2,3584]{2,1,0:T(2,128)(2,1)} reshape(bf16[256,56,128]{2,1,0:T(8,128)(2,1)} %convert_bitcast_fusion) | data formatting | bytes 7340032 | tf_op jit(solution)/shard_map/reshape | solution.py:42
  256.3 167.1 %all-reduce.2.cloned.1.call-done = f32[128,128,128]{2,1,0:T(8,128)} async-done(((f32[128,128,128]{2,1,0:T(8,128)}), f32[128,128,128]{2,1,0:T(8,128)}) %all-reduce.2.cloned.1.call-update) | async-done | bytes 8388624 | tf_op jit(solution)/shard_map/psum | solution.py:53
  423.4 4.0 gather_fusion.2
  427.4 0.9 fusion.9
  (21 shorter events, 0.3 us)
Async XLA Ops:
  7.2 170.0 %all-gather.2.cloned.1.call-start = ((), (), s32[]{:S(2)}) async-start(), calls=%async_computation.1 | async-start | bytes 4718592 | tf_op jit(solution)/shard_map/all_gather | solution.py:29
  42.9 21.1 %copy-start.2 = (s32[128]{0:T(128)S(1)}, s32[128]{0:T(128)}, u32[]{:S(2)}) copy-start(s32[128]{0:T(128)} %param.10) | copy-start | bytes 1540
  42.9 21.1 %copy-start.1 = (s32[128]{0:T(128)S(1)}, s32[128]{0:T(128)}, u32[]{:S(2)}) copy-start(s32[128]{0:T(128)} %param.11) | copy-start | bytes 1540
  59.4 48.6 %all-to-all-start = ((bf16[8,2,114688]{2,1,0:T(2,128)(2,1)}), bf16[8,2,114688]{2,1,0:T(2,128)(2,1)}, u32[]{:S(2)}, u32[]{:S(2)}) async-start(bf16[8,2,114688]{2,1,0:T(2,128)(2,1)} %reshape.95), calls=%async_computation | async-start | bytes 7340032 | tf_op jit(solution)/shard_map/all_to_all | solution.py:18
  63.9 359.5 %all-reduce.2.cloned.1.call-start = ((), (), s32[]{:S(2)}) async-start(), calls=%async_computation.2 | async-start | bytes 16777216 | tf_op jit(solution)/shard_map/psum | solution.py:53
  210.6 0.7 copy-start
Sparse Core Ops, SparseCore 0:
  9.8 37.5 all-gather.1
  210.7 212.6 all-reduce.1
where the time goes:
time: 440 us; the launch traced here: 435 us
  waiting for transfers between devices  212 us (48%)
  local copies, waits for them, and re-layouts  154 us (35%)
  matrix products  48 us (11%)
  between operations  14.8 us (3%)
  starting transfers between devices  4.57 us (1%)
    psum x1, waiting for transfers between devices, local(): summed = lax.psum(grad_sum, 'dp')  167 us
    unnamed x9, local copies, waits for them, and re-layouts  63.1 us
    all_to_all x1, waiting for transfers between devices, local(): lax.all_to_all(upstream, 'mp', split_axis=2, concat_axis=0, tiled=True)  43.9 us
    all_to_all x1, local copies, waits for them, and re-layouts, local(): lax.all_to_all(upstream, 'mp', split_axis=2, concat_axis=0, tiled=True)  35 us
    dot_general x1, matrix products, local(): jnp.einsum('kc,kno->cno', column_table, product, precision=lax.Precision....  22.5 us
    reshape x2, local copies, waits for them, and re-layouts, local(): hidden.reshape(group_rows, column_blocks, tile_size)  14 us
    dot_general x1, matrix products, local(): jnp.einsum('kni,kio->kno', feature_tiles, deltas, preferred_element_type=...  13.6 us
    dot_general x1, matrix products, local(): jnp.einsum('kni,kno->kio', feature_tiles, upstream_chosen, preferred_elem...  11.9 us
  transfers between devices with their start and end apart: 3, of which 2 were waited for; matrix products, arithmetic and copies ran while one was open for 38% of the time, Pallas kernels for 0%

commit v1 on v0

v1 whole, which is shorter than its diff:
```python
import jax
import jax.numpy as jnp
from jax import lax
from jax.sharding import PartitionSpec as P


def owner_slots(block_owner, live_slots, dp_count, owner_cap):
    owner_hot = (
        (block_owner[:, None] == jnp.arange(dp_count, dtype=jnp.int32)[None, :])
        & live_slots[:, None]
    ).astype(jnp.int32)
    before = jnp.cumsum(owner_hot, axis=0) - owner_hot
    owner_rank = jnp.sum(before * owner_hot, axis=1)
    targets = block_owner * owner_cap + owner_rank
    slot_ids = jnp.arange(dp_count * owner_cap, dtype=jnp.int32)
    chosen = live_slots[None, :] & (targets[None, :] == slot_ids[:, None])
    entry_ids = jnp.arange(block_owner.shape[0], dtype=jnp.int32)
    source_index = jnp.sum(jnp.where(chosen, entry_ids[None, :], 0), axis=1).astype(jnp.int32)
    present = jnp.any(chosen, axis=1)
    return source_index, present


def gather_columns(upstream, mp_count):
    me = lax.axis_index("mp")
    width = upstream.shape[2] // mp_count
    pieces = [None] * mp_count
    for shift in range(mp_count):
        target = (me + shift) % mp_count
        piece = lax.dynamic_slice_in_dim(upstream, target * width, width, 2)
        if shift:
            perm = [(m, (m + shift) % mp_count) for m in range(mp_count)]
            piece = lax.ppermute(piece, "mp", perm)
        pieces[shift] = piece
    stacked = jnp.stack(pieces, axis=0)
    shift_of_source = (me - jnp.arange(mp_count, dtype=jnp.int32)) % mp_count
    ordered = jnp.take(stacked, shift_of_source, axis=0)
    return ordered.reshape((mp_count * upstream.shape[0],) + upstream.shape[1:2] + (width,))


def local(tokens, upstream, deltas, block_row, block_column, block_owner, block_count):
    model_width = tokens.shape[1]
    tile_size = deltas.shape[1]
    slot_count = deltas.shape[0]
    mp_count = lax.axis_size("mp")
    dp_count = lax.axis_size("dp")
    hidden = gather_columns(upstream, mp_count)
    group_rows = hidden.shape[0]
    column_blocks = hidden.shape[1] * hidden.shape[2] // tile_size
    hidden_major = jnp.transpose(hidden.reshape(group_rows, column_blocks, tile_size), (1, 0, 2))
    upstream_chosen = jnp.take(hidden_major, block_column, axis=0)
    slot_ids = jnp.arange(slot_count, dtype=jnp.int32)
    live_slots = slot_ids < block_count[0]
    column_table = (
        live_slots[:, None]
        & (block_column[:, None] == jnp.arange(column_blocks, dtype=jnp.int32)[None, :])
    ).astype(jnp.float32)
    shard_rows = lax.all_gather(tokens, "mp", axis=0, tiled=True)
    row_count = shard_rows.shape[0]
    row_major = jnp.transpose(
        shard_rows.reshape(row_count, model_width // tile_size, tile_size), (1, 0, 2)
    )
    feature_tiles = jnp.take(row_major, block_row, axis=0)
    grad_sum = jnp.einsum(
        "kni,kno->kio", feature_tiles, upstream_chosen, preferred_element_type=jnp.float32
    )
    owner_cap = 3 * slot_count // (2 * dp_count)
    source_index, present = owner_slots(block_owner, live_slots, dp_count, owner_cap)
    by_slot = jnp.where(present[:, None, None], jnp.take(grad_sum, source_index, axis=0), 0.0)
    owned = lax.psum_scatter(by_slot, "dp", scatter_dimension=0, tiled=True)
    product = jnp.einsum("kni,kio->kno", feature_tiles, deltas, preferred_element_type=jnp.float32)
    rows_out = jnp.einsum("kc,kno->cno", column_table, product, precision=lax.Precision.HIGHEST)
    branch_out = jnp.transpose(rows_out.astype(jnp.bfloat16), (1, 0, 2)).reshape(
        group_rows, hidden.shape[1], hidden.shape[2]
    )
    return (branch_out, owned[None])


def solution(mesh):
    placed = (
        P(("dp", "mp"), None),
        P(("dp", "mp"), None, None),
        P("mp", None, None),
        P("mp"),
        P("mp"),
        P("mp"),
        P("mp"),
    )
    return jax.shard_map(
        local,
        mesh=mesh,
        in_specs=placed,
        out_specs=(P("dp", None, "mp"), P("mp", "dp", None, None)),
        check_vma=False,
    )
```

time: 440 us -> 425 us (0.966)
  local copies, waits for them, and re-layouts: 154 us -> 87.6 us
  starting transfers between devices: 4.57 us -> 26.1 us
  other arithmetic: 1.61 us -> 16.5 us
  waiting for transfers between devices: 212 us -> 224 us
    reduce_scatter x0 -> x1, waiting for transfers between devices: none -> 199 us  [local(): owned = lax.psum_scatter(by_slot, 'dp', scatter_dimension=0, tiled=True)]
    psum x1 -> x0, waiting for transfers between devices: 167 us -> none  [local(): summed = lax.psum(grad_sum, 'dp')]
    unnamed x9 -> x13, local copies, waits for them, and re-layouts: 63.1 us -> 8.61 us
    all_to_all x1 -> x0, waiting for transfers between devices: 43.9 us -> none  [local(): lax.all_to_all(upstream, 'mp', split_axis=2, concat_axis=0, tiled=True)]
    all_to_all x1 -> x0, local copies, waits for them, and re-layouts: 35 us -> none  [local(): lax.all_to_all(upstream, 'mp', split_axis=2, concat_axis=0, tiled=True)]
    gather x1 -> x3, local copies, waits for them, and re-layouts: 3.95 us -> 34.5 us  [the longest x2 20.5 us: gather_columns(): ordered = jnp.take(stacked, shift_of_source, axis=0)]
    ppermute x0 -> x7, starting transfers between devices: none -> 26 us  [gather_columns(): piece = lax.ppermute(piece, 'mp', perm)]
    ppermute x0 -> x7, waiting for transfers between devices: none -> 24.4 us  [gather_columns(): piece = lax.ppermute(piece, 'mp', perm)]
  transfers between devices with their start and end apart: 3 -> 9, of which waited for: 2 -> 5; matrix products, arithmetic and copies ran while one was open for 38% -> 22% of each run, Pallas kernels for 0% -> 0%
where the time goes in v1:
time: 425 us; the launch traced here: 418 us
  waiting for transfers between devices  224 us (53%)
  local copies, waits for them, and re-layouts  87.6 us (21%)
  matrix products  47.7 us (11%)
  starting transfers between devices  26.1 us (6%)
  other arithmetic  16.5 us (4%)
  between operations  15.4 us (4%)
    reduce_scatter x1, waiting for transfers between devices, local(): owned = lax.psum_scatter(by_slot, 'dp', scatter_dimension=0, tiled=True)  199 us
    ppermute x7, starting transfers between devices, gather_columns(): piece = lax.ppermute(piece, 'mp', perm)  26 us
    ppermute x7, waiting for transfers between devices, gather_columns(): piece = lax.ppermute(piece, 'mp', perm)  24.4 us
    dot_general x1, matrix products, local(): jnp.einsum('kc,kno->cno', column_table, product, precision=lax.Precision....  23.1 us
    gather x2, local copies, waits for them, and re-layouts, gather_columns(): ordered = jnp.take(stacked, shift_of_source, axis=0)  20.5 us
    gather x1, local copies, waits for them, and re-layouts, local(): jnp.take(grad_sum, source_index, axis=0)  14 us
    dot_general x1, matrix products, local(): jnp.einsum('kni,kio->kno', feature_tiles, deltas, preferred_element_type=...  12.7 us
    dot_general x1, matrix products, local(): jnp.einsum('kni,kno->kio', feature_tiles, upstream_chosen, preferred_elem...  11.9 us
  transfers between devices with their start and end apart: 9, of which 5 were waited for; matrix products, arithmetic and copies ran while one was open for 22% of the time, Pallas kernels for 0%

profile of v1, /device:TPU:6, one launch (start us, length us, event | category | flops | bytes accessed | tf_op | source)
XLA Modules:
  0.0 417.7 jit_solution(4054217540737102702)
XLA Ops:
  8.1 4.7 %constant_dynamic-slice_fusion = (bf16[32,2,3584]{2,1,0:T(2,128)(2,1)S(1)}, bf16[32,2,3584]{2,1,0:T(2,128)(2,1)}, bf16[32,2,3584]{2,1,0:T(2,128)(2,1)}, bf16[32,...) fusion(bf16[32,2,28672]{2,1,0:T(2,128)(2,1)} %param.8, ...), kind=kLoop, calls=%fused_computation.51 | loop fusion | bytes 6422556 | tf_op jit(solution)/shard_map/dynamic_slice | solution.py:29
  14.4 2.2 collective-permute-start.2
  16.6 1.8 collective-permute-start.3
  18.4 1.8 collective-permute-start.4
  22.0 2.1 bitcast_dynamic-update-slice_fusion.7
  24.1 2.2 collective-permute-done
  26.3 1.8 collective-permute-start.5
  29.2 16.7 %collective-permute-start.6 = (bf16[32,2,3584]{2,1,0:T(2,128)(2,1)S(1)}, bf16[32,2,3584]{2,1,0:T(2,128)(2,1)S(1)}, u32[]{:S(2)}, u32[]{:S(2)}) collective-permute-start(bf16[32,2,3584]{2,1,0:T(2,128)(2,1)S(1)} %get-tuple-element.2), channel_id=1, source_target_pairs={{0,7},{1,0},{2,1},{3,2},{4,3},{5,4},{6,5},{7,6},{8,15},{9,8},{10,9... | collective-permute-start | bytes 1376264 | tf_op jit(solution)/shard_map/ppermute | solution.py:32
  47.0 17.1 %collective-permute-done.2 = bf16[32,2,3584]{2,1,0:T(2,128)(2,1)S(1)} collective-permute-done((bf16[32,2,3584]{2,1,0:T(2,128)(2,1)}, bf16[32,2,3584]{2,1,0:T(2,128)(2,1)S(1)}, u32[]{:S(2)}, u32[]{:S(2)}) %collective-permute-start.2) | collective-permute-done | bytes 458784 | tf_op jit(solution)/shard_map/ppermute | solution.py:32
  66.5 4.8 %collective-permute-done.4 = bf16[32,2,3584]{2,1,0:T(2,128)(2,1)S(1)} collective-permute-done((bf16[32,2,3584]{2,1,0:T(2,128)(2,1)}, bf16[32,2,3584]{2,1,0:T(2,128)(2,1)S(1)}, u32[]{:S(2)}, u32[]{:S(2)}) %collective-permute-start.4) | collective-permute-done | bytes 458784 | tf_op jit(solution)/shard_map/ppermute | solution.py:32
  74.6 11.4 %gather_fusion.1 = bf16[8,32,2,3584]{3,2,1,0:T(2,128)(2,1)} fusion(bf16[8,32,2,3584]{3,2,1,0:T(2,128)(2,1)} %bitcast_dynamic-update-slice_fusion, s32[1024]{0:T(1024)S(1)} %pad_clamp_fusion.2), kind=kCustom, calls=%fused_computation.1 | custom fusion | bytes 7340064 | tf_op jit(solution)/shard_map/jit(_take)/gather | solution.py:36
  85.9 9.2 %gather.20 = bf16[256,56,128]{2,1,0:T(8,128)(2,1)} reshape(bf16[8,32,2,3584]{3,2,1,0:T(2,128)(2,1)} %gather_fusion.1) | data formatting | bytes 7340032 | tf_op jit(solution)/shard_map/jit(_take)/gather | solution.py:36
  95.1 4.4 %fusion.6 = bf16[56,256,128]{2,1,0:T(8,128)(2,1)} fusion(bf16[256,56,128]{2,1,0:T(8,128)(2,1)} %gather.20, pred[256]{0:T(512)(128)(4,1)S(1)} %broadcast_in_dim.93), kind=kLoop, calls=%fused_computation.13 | loop fusion | flops 1835008 | bytes 7340288 | tf_op jit(solution)/shard_map/transpose | solution.py:49
  99.5 8.6 %gather_fusion.2 = bf16[128,256,128]{2,1,0:T(8,128)(2,1)} fusion(bf16[56,256,128]{2,1,0:T(8,128)(2,1)} %fusion.6, s32[1024]{0:T(1024)S(1)} %pad_clamp_fusion.1), kind=kCustom, calls=%fused_computation.2 | custom fusion | bytes 16777728 | tf_op jit(solution)/shard_map/jit(_take)/gather | solution.py:50
  108.1 6.4 %copy.21 = bf16[256,8192]{0,1:T(8,128)(2,1)} copy(bf16[256,8192]{1,0:T(8,128)(2,1)} %all-gather.2.cloned.1.call-done) | data formatting | bytes 8388608 | tf_op jit(solution)/shard_map/all_gather | solution.py:57
  114.5 6.3 %copy.22 = bf16[256,64,128]{2,0,1:T(8,128)(2,1)} copy(bf16[256,64,128]{0,2,1:T(8,128)(2,1)} %bitcast.34) | data formatting | bytes 8388608 | tf_op jit(solution)/shard_map/reshape | solution.py:60
  120.8 9.1 %gather_fusion = bf16[128,256,128]{2,1,0:T(8,128)(2,1)} fusion(bf16[64,256,128]{2,1,0:T(8,128)(2,1)} %bitcast.33, s32[1024]{0:T(1024)S(1)} %pad_clamp_fusion.3), kind=kCustom, calls=%fused_computation | custom fusion | bytes 16777728 | tf_op jit(solution)/shard_map/jit(_take)/gather | solution.py:62
  129.9 11.9 %fusion.2 = f32[128,128,128]{2,1,0:T(8,128)} fusion(bf16[128,256,128]{2,1,0:T(8,128)(2,1)} %gather_fusion.2, pred[128]{0:T(512)(128)(4,1)S(1)} %get-tuple-element.11, bf16[128,256,128]{2,1,0:T(8,128)(2,1)} %gather_fusion, pred[128]{0:T(512)(128)(4,1)S(1)} %get-tuple-element.12), kind=kOutput, calls=%fused_computation.7 | convolution fusion | flops 1082130432 | bytes 25166080 | tf_op jit(solution)/shard_map/kni,kno->kio/dot_general | solution.py:63
  141.8 14.0 %gather_fusion.3 = f32[192,128,128]{2,1,0:T(8,128)} fusion(f32[128,128,128]{2,1,0:T(8,128)} %fusion.2, s32[1024]{0:T(1024)S(1)} %pad_clamp_fusion), kind=kCustom, calls=%fused_computation.3 | custom fusion | bytes 25166592 | tf_op jit(solution)/shard_map/jit(_take)/gather | solution.py:68
  155.8 11.3 %select_select_fusion = f32[192,128,128]{2,1,0:T(8,128)} fusion(f32[192,128,128]{2,1,0:T(8,128)} %gather_fusion.3, pred[192]{0:T(512)(128)(4,1)S(1)} %compare_and_fusion.2, pred[192]{0:T(512)(128)(4,1)S(1)} %fusion.11), kind=kLoop, calls=%fused_computation.6 | loop fusion | flops 6291456 | bytes 25166208 | tf_op jit(solution)/shard_map/jit(_where)/select_n | solution.py:68
  167.1 12.7 %fusion.7 = f32[128,256,128]{2,1,0:T(8,128)} fusion(bf16[128,128,128]{2,1,0:T(8,128)(2,1)} %param.9, bf16[128,256,128]{2,1,0:T(8,128)(2,1)} %gather_fusion, pred[128]{0:T(512)(128)(4,1)S(1)} %get-tuple-element.12), kind=kOutput, calls=%fused_computation.15 | convolution fusion | flops 1077936128 | bytes 29360256 | tf_op jit(solution)/shard_map/kni,kio->kno/dot_general | solution.py:70
  179.8 23.1 %convert_bitcast_fusion = bf16[256,56,128]{2,1,0:T(8,128)(2,1)} fusion(f32[128,256,128]{2,1,0:T(8,128)} %fusion.7, s32[128]{0:T(128)S(1)} %copy-done, pred[128]{0:T(512)(128)(4,1)S(1)} %iota_compare_fusion.3), kind=kOutput, calls=%fused_computation.14 | convolution fusion | flops 2820421632 | bytes 20447872 | tf_op jit(solution)/shard_map/kc,kno->cno/dot_general | solution.py:71
  202.9 8.1 %reshape.107 = bf16[256,2,3584]{2,1,0:T(2,128)(2,1)} reshape(bf16[256,56,128]{2,1,0:T(8,128)(2,1)} %convert_bitcast_fusion) | data formatting | bytes 7340032 | tf_op jit(solution)/shard_map/reshape | solution.py:72
  211.0 199.4 %reduce-scatter.2.cloned.1.call-done = f32[6,128,128]{2,1,0:T(8,128)} async-done(((f32[192,128,128]{2,1,0:T(8,128)}), f32[6,128,128]{2,1,0:T(8,128)}) %reduce-scatter.2.cloned.1.call-update) | async-done | bytes 393232 | tf_op jit(solution)/shard_map/reduce_scatter | solution.py:69
  (43 shorter events, 11.2 us)
Async XLA Ops:
  7.2 13.1 %copy-start = (s32[128]{0:T(128)S(1)}, s32[128]{0:T(128)}, u32[]{:S(2)}) copy-start(s32[128]{0:T(128)} %param.11) | copy-start | bytes 1540
  7.2 13.1 %copy-start.2 = (s32[128]{0:T(128)S(1)}, s32[128]{0:T(128)}, u32[]{:S(2)}) copy-start(s32[128]{0:T(128)} %param.10) | copy-start | bytes 1540
  7.2 13.8 %copy-start.1 = (s32[128]{0:T(128)S(1)}, s32[128]{0:T(128)}, u32[]{:S(2)}) copy-start(s32[128]{0:T(128)} %param.12) | copy-start | bytes 1540
  7.2 100.9 %all-gather.2.cloned.1.call-start = ((), (), s32[]{:S(2)}) async-start(), calls=%async_computation.1 | async-start | bytes 4718592 | tf_op jit(solution)/shard_map/all_gather | solution.py:57
  7.9 402.5 %reduce-scatter.2.cloned.1.call-start = ((), (), s32[]{:S(2)}) async-start(), calls=%async_computation.2 | async-start | bytes 12976128 | tf_op jit(solution)/shard_map/reduce_scatter | solution.py:69
  12.7 13.6 %collective-permute-start = (bf16[32,2,3584]{2,1,0:T(2,128)(2,1)}, bf16[32,2,3584]{2,1,0:T(2,128)(2,1)S(1)}, u32[]{:S(2)}, u32[]{:S(2)}) collective-permute-start(bf16[32,2,3584]{2,1,0:T(2,128)(2,1)} %get-tuple-element.7), channel_id=1, source_target_pairs={{0,1},{1,2},{2,3},{3,4},{4,5},{5,6},{6,7},{7,0},{8,9},{9,10},{10,1... | collective-permute-start | bytes 1376264 | tf_op jit(solution)/shard_map/ppermute | solution.py:32
  12.7 16.5 %collective-permute-start.1 = (bf16[32,2,3584]{2,1,0:T(2,128)(2,1)}, bf16[32,2,3584]{2,1,0:T(2,128)(2,1)S(1)}, u32[]{:S(2)}, u32[]{:S(2)}) collective-permute-start(bf16[32,2,3584]{2,1,0:T(2,128)(2,1)} %get-tuple-element.6), channel_id=1, source_target_pairs={{0,2},{1,3},{2,4},{3,5},{4,6},{5,7},{6,0},{7,1},{8,10},{9,11},{10,... | collective-permute-start | bytes 1376264 | tf_op jit(solution)/shard_map/ppermute | solution.py:32
  14.4 49.7 %collective-permute-start.2 = (bf16[32,2,3584]{2,1,0:T(2,128)(2,1)}, bf16[32,2,3584]{2,1,0:T(2,128)(2,1)S(1)}, u32[]{:S(2)}, u32[]{:S(2)}) collective-permute-start(bf16[32,2,3584]{2,1,0:T(2,128)(2,1)} %get-tuple-element.5), channel_id=1, source_target_pairs={{0,3},{1,4},{2,5},{3,6},{4,7},{5,0},{6,1},{7,2},{8,11},{9,12},{10,... | collective-permute-start | bytes 1376264 | tf_op jit(solution)/shard_map/ppermute | solution.py:32
  16.6 48.8 %collective-permute-start.3 = (bf16[32,2,3584]{2,1,0:T(2,128)(2,1)}, bf16[32,2,3584]{2,1,0:T(2,128)(2,1)S(1)}, u32[]{:S(2)}, u32[]{:S(2)}) collective-permute-start(bf16[32,2,3584]{2,1,0:T(2,128)(2,1)} %get-tuple-element.4), channel_id=1, source_target_pairs={{0,4},{1,5},{2,6},{3,7},{4,0},{5,1},{6,2},{7,3},{8,12},{9,13},{10,... | collective-permute-start | bytes 1376264 | tf_op jit(solution)/shard_map/ppermute | solution.py:32
  18.4 52.9 %collective-permute-start.4 = (bf16[32,2,3584]{2,1,0:T(2,128)(2,1)}, bf16[32,2,3584]{2,1,0:T(2,128)(2,1)S(1)}, u32[]{:S(2)}, u32[]{:S(2)}) collective-permute-start(bf16[32,2,3584]{2,1,0:T(2,128)(2,1)} %get-tuple-element.3), channel_id=1, source_target_pairs={{0,5},{1,6},{2,7},{3,0},{4,1},{5,2},{6,3},{7,4},{8,13},{9,14},{10,... | collective-permute-start | bytes 1376264 | tf_op jit(solution)/shard_map/ppermute | solution.py:32
  26.3 46.1 %collective-permute-start.5 = (bf16[32,2,3584]{2,1,0:T(2,128)(2,1)S(1)}, bf16[32,2,3584]{2,1,0:T(2,128)(2,1)S(1)}, u32[]{:S(2)}, u32[]{:S(2)}) collective-permute-start(bf16[32,2,3584]{2,1,0:T(2,128)(2,1)S(1)} %get-tuple-element.8), channel_id=1, source_target_pairs={{0,6},{1,7},{2,0},{3,1},{4,2},{5,3},{6,4},{7,5},{8,14},{9,15},{10,... | collective-permute-start | bytes 1376264 | tf_op jit(solution)/shard_map/ppermute | solution.py:32
  29.2 44.3 %collective-permute-start.6 = (bf16[32,2,3584]{2,1,0:T(2,128)(2,1)S(1)}, bf16[32,2,3584]{2,1,0:T(2,128)(2,1)S(1)}, u32[]{:S(2)}, u32[]{:S(2)}) collective-permute-start(bf16[32,2,3584]{2,1,0:T(2,128)(2,1)S(1)} %get-tuple-element.2), channel_id=1, source_target_pairs={{0,7},{1,0},{2,1},{3,2},{4,3},{5,4},{6,5},{7,6},{8,15},{9,8},{10,9... | collective-permute-start | bytes 1376264 | tf_op jit(solution)/shard_map/ppermute | solution.py:32
Sparse Core Ops, SparseCore 0:
  9.9 66.7 all-gather.1
  167.3 243.1 reduce-scatter.1

commit v2 on v1

--- a/solution.py
+++ b/solution.py
@@ -4,20 +4,118 @@
 from jax.sharding import PartitionSpec as P
 
 
-def owner_slots(block_owner, live_slots, dp_count, owner_cap):
+def owner_ranks(block_owner, live_slots, dp_count):
     owner_hot = (
         (block_owner[:, None] == jnp.arange(dp_count, dtype=jnp.int32)[None, :])
         & live_slots[:, None]
     ).astype(jnp.int32)
     before = jnp.cumsum(owner_hot, axis=0) - owner_hot
-    owner_rank = jnp.sum(before * owner_hot, axis=1)
-    targets = block_owner * owner_cap + owner_rank
-    slot_ids = jnp.arange(dp_count * owner_cap, dtype=jnp.int32)
-    chosen = live_slots[None, :] & (targets[None, :] == slot_ids[:, None])
-    entry_ids = jnp.arange(block_owner.shape[0], dtype=jnp.int32)
+    return jnp.sum(before * owner_hot, axis=1)
+
+
+def slot_sources(targets, selected, slot_total):
+    slot_ids = jnp.arange(slot_total, dtype=jnp.int32)
+    chosen = selected[None, :] & (targets[None, :] == slot_ids[:, None])
+    entry_ids = jnp.arange(targets.shape[0], dtype=jnp.int32)
     source_index = jnp.sum(jnp.where(chosen, entry_ids[None, :], 0), axis=1).astype(jnp.int32)
-    present = jnp.any(chosen, axis=1)
-    return source_index, present
+    return source_index, jnp.any(chosen, axis=1)
+
+
+def local_part(table, keep, size_of_chunk):
+    def part(c, h):
+        rows = lax.dynamic_slice_in_dim(table, c * size_of_chunk, size_of_chunk, 0)[:, h]
+        if keep is None:
+            return rows
+        mask = lax.dynamic_slice_in_dim(keep, c * size_of_chunk, size_of_chunk, 0)
+        return jnp.where(mask[:, None, None], rows, 0.0)
+    return part
+
+
+def reduce_owned(grad_sum, block_owner, live_slots, dp_count, owner_cap, row_len, pieces):
+    x_count = dp_count // row_len
+    half_cap = owner_cap // 2
+    rank = owner_ranks(block_owner, live_slots, dp_count)
+    owner_x = block_owner // row_len
+    owner_z = block_owner % row_len
+    half_slots = dp_count * half_cap
+    in_a = live_slots & (rank < half_cap)
+    in_b = live_slots & (rank >= half_cap)
+    target_a = owner_z * (x_count * half_cap) + owner_x * half_cap + rank
+    target_b = owner_x * (row_len * half_cap) + owner_z * half_cap + rank - half_cap
+    source_a, keep_a = slot_sources(target_a, in_a, half_slots)
+    source_b, keep_b = slot_sources(target_b, in_b, half_slots)
+    tile = grad_sum.shape[1]
+    gathered = jnp.take(grad_sum, jnp.concatenate([source_a, source_b]), axis=0)
+    gathered = gathered.reshape((2, half_slots, 2, tile // 2) + grad_sum.shape[2:])
+    table_a, table_b = gathered[0], gathered[1]
+
+    dp_me = lax.axis_index("dp")
+    me_z = dp_me % row_len
+    me_x = dp_me // row_len
+
+    def z_perm(shift):
+        return [(i, (i // row_len) * row_len + (i % row_len + shift) % row_len) for i in range(dp_count)]
+
+    def x_perm(shift):
+        return [(i, (i + shift * row_len) % dp_count) for i in range(dp_count)]
+
+    z_ring = (row_len, me_z, z_perm)
+    x_ring = (x_count, me_x, x_perm)
+    plan_a = [(z_ring, local_part(table_a, keep_a, x_count * half_cap)), (x_ring, None)]
+    plan_b = [(x_ring, local_part(table_b, keep_b, row_len * half_cap)), (z_ring, None)]
+
+    def start(ring, part):
+        size, me, _ = ring
+        return [part((me - 1) % size, 0), part((me + 1) % size, 1)]
+
+    def finish(halves):
+        return jnp.concatenate([halves[0], halves[1]], axis=1)
+
+    def second_part(row_sum):
+        def part(c, h):
+            rows = lax.dynamic_slice_in_dim(row_sum, c * half_cap, half_cap, 0)
+            return rows[:, h * (tile // 2):(h + 1) * (tile // 2)]
+        return part
+
+    rings = [plan_a, plan_b]
+    states = []
+    for plan in rings:
+        (ring1, part1), _ = plan
+        states.append({"stage": 0, "k": 0, "halves": start(ring1, part1), "part": part1})
+    total_steps = max((p[0][0][0] - 1) + (p[1][0][0] - 1) for p in rings)
+    tie_at = {max(1, (total_steps * (i + 1)) // (len(pieces) + 1)): i for i in range(len(pieces))}
+    results = [None] * len(pieces)
+    for step in range(total_steps):
+        received = []
+        for plan, st in zip(rings, states):
+            ring = plan[st["stage"]][0]
+            received.append([
+                lax.ppermute(st["halves"][0], "dp", ring[2](1)),
+                lax.ppermute(st["halves"][1], "dp", ring[2](-1)),
+            ])
+        if step in tie_at:
+            index = tie_at[step]
+            received, results[index] = lax.optimization_barrier((received, pieces[index]()))
+        for plan, st, got in zip(rings, states, received):
+            size, me, _ = plan[st["stage"]][0]
+            k = st["k"]
+            part = st["part"]
+            st["halves"] = [
+                got[0] + part((me - k - 2) % size, 0),
+                got[1] + part((me + k + 2) % size, 1),
+            ]
+            st["k"] = k + 1
+            if st["k"] == size - 1 and st["stage"] == 0:
+                row_sum = finish(st["halves"])
+                ring2 = plan[1][0]
+                st["stage"], st["k"] = 1, 0
+                st["part"] = second_part(row_sum)
+                st["halves"] = start(ring2, st["part"])
+    for index in range(len(pieces)):
+        if results[index] is None:
+            results[index] = pieces[index]()
+    owned = jnp.concatenate([finish(states[0]["halves"]), finish(states[1]["halves"])], axis=0)
+    return owned, results
 
 
 def gather_columns(upstream, mp_count):
@@ -64,14 +162,25 @@
         "kni,kno->kio", feature_tiles, upstream_chosen, preferred_element_type=jnp.float32
     )
     owner_cap = 3 * slot_count // (2 * dp_count)
-    source_index, present = owner_slots(block_owner, live_slots, dp_count, owner_cap)
-    by_slot = jnp.where(present[:, None, None], jnp.take(grad_sum, source_index, axis=0), 0.0)
-    owned = lax.psum_scatter(by_slot, "dp", scatter_dimension=0, tiled=True)
-    product = jnp.einsum("kni,kio->kno", feature_tiles, deltas, preferred_element_type=jnp.float32)
-    rows_out = jnp.einsum("kc,kno->cno", column_table, product, precision=lax.Precision.HIGHEST)
-    branch_out = jnp.transpose(rows_out.astype(jnp.bfloat16), (1, 0, 2)).reshape(
-        group_rows, hidden.shape[1], hidden.shape[2]
-    )
+    row_len = 8 if dp_count % 8 == 0 else dp_count
+    piece_count = 4
+    piece_rows = group_rows // piece_count
+
+    def branch_piece(i):
+        def run():
+            rows_in = feature_tiles[:, i * piece_rows:(i + 1) * piece_rows]
+            product = jnp.einsum("kni,kio->kno", rows_in, deltas, preferred_element_type=jnp.float32)
+            rows_out = jnp.einsum("kc,kno->cno", column_table, product, precision=lax.Precision.HIGHEST)
+            return jnp.transpose(rows_out.astype(jnp.bfloat16), (1, 0, 2)).reshape(
+                piece_rows, hidden.shape[1], hidden.shape[2]
+            )
+        return run
+
+    owned, branch_parts = reduce_owned(
+        grad_sum, block_owner, live_slots, dp_count, owner_cap, row_len,
+        [branch_piece(i) for i in range(piece_count)],
+    )
+    branch_out = jnp.concatenate(branch_parts, axis=0)
     return (branch_out, owned[None])
 
 

time: 425 us -> 392 us (0.922)
  waiting for transfers between devices: 224 us -> 88.8 us
  starting transfers between devices: 26.1 us -> 72.7 us
  other arithmetic: 16.5 us -> 60.3 us
  local copies, waits for them, and re-layouts: 87.6 us -> 101 us
    reduce_scatter x1 -> x0, waiting for transfers between devices: 199 us -> none  [local(): owned = lax.psum_scatter(by_slot, 'dp', scatter_dimension=0, tiled=True)]
    ppermute x0 -> x40, starting transfers between devices: none -> 57.4 us  [the longest x20 31.1 us: reduce_owned(): lax.ppermute(st['halves'][1], 'dp', ring[2](-1))]
    ppermute x0 -> x40, waiting for transfers between devices: none -> 39.1 us  [the longest x20 27.6 us: reduce_owned(): lax.ppermute(st['halves'][1], 'dp', ring[2](-1))]
    add x1 -> x27, other arithmetic: 0.01 us -> 26.5 us  [the longest x18 21.1 us: reduce_owned(): got[1] + part((me + k + 2) % size, 1)]
    ppermute x7, waiting for transfers between devices: 24.4 us -> 49 us  [gather_columns(): piece = lax.ppermute(piece, 'mp', perm)]
    ppermute x7, starting transfers between devices: 26 us -> 15.3 us  [gather_columns(): piece = lax.ppermute(piece, 'mp', perm)]
    select_n x2 -> x5, other arithmetic: 11.3 us -> 20.2 us  [the longest x2 10.1 us: reduce_owned(): gathered = jnp.take(grad_sum, jnp.concatenate([source_a, source_b]), axis=0)]
    slice x0 -> x1, local copies, waits for them, and re-layouts: none -> 8.81 us  [reduce_owned(): table_a, table_b = (gathered[0], gathered[1])]
  transfers between devices with their start and end apart: 9 -> 48, of which waited for: 5 -> 15; matrix products, arithmetic and copies ran while one was open for 22% -> 32% of each run, Pallas kernels for 0% -> 0%
where the time goes in v2:
time: 392 us; the launch traced here: 385 us
  local copies, waits for them, and re-layouts  101 us (26%)
  waiting for transfers between devices  88.8 us (23%)
  starting transfers between devices  72.7 us (19%)
  other arithmetic  60.3 us (15%)
  matrix products  46.8 us (12%)
  between operations  15.7 us (4%)
    ppermute x7, waiting for transfers between devices, gather_columns(): piece = lax.ppermute(piece, 'mp', perm)  49 us
    ppermute x20, starting transfers between devices, reduce_owned(): lax.ppermute(st['halves'][1], 'dp', ring[2](-1))  31.1 us
    ppermute x20, waiting for transfers between devices, reduce_owned(): lax.ppermute(st['halves'][1], 'dp', ring[2](-1))  27.6 us
    ppermute x20, starting transfers between devices, reduce_owned(): lax.ppermute(st['halves'][0], 'dp', ring[2](1))  26.3 us
    add x18, other arithmetic, reduce_owned(): got[1] + part((me + k + 2) % size, 1)  21.1 us
    gather x2, local copies, waits for them, and re-layouts, gather_columns(): ordered = jnp.take(stacked, shift_of_source, axis=0)  20.8 us
    dot_general x4, matrix products, run(): jnp.einsum('kc,kno->cno', column_table, product, precision=lax.Precision....  19.1 us
    dot_general x4, matrix products, run(): jnp.einsum('kni,kio->kno', rows_in, deltas, preferred_element_type=jnp.fl...  16 us
  transfers between devices with their start and end apart: 48, of which 15 were waited for; matrix products, arithmetic and copies ran while one was open for 32% of the time, Pallas kernels for 0%

profile of v2, /device:TPU:6, one launch (start us, length us, event | category | flops | bytes accessed | tf_op | source)
XLA Modules:
  0.0 384.9 jit_solution(3544647587624599840)
XLA Ops:
  8.0 4.6 %constant_dynamic-slice_fusion = (bf16[32,2,3584]{2,1,0:T(2,128)(2,1)S(1)}, bf16[32,2,3584]{2,1,0:T(2,128)(2,1)}, bf16[32,2,3584]{2,1,0:T(2,128)(2,1)}, bf16[32,...) fusion(bf16[32,2,28672]{2,1,0:T(2,128)(2,1)} %param.8, ...), kind=kLoop, calls=%fused_computation.221 | loop fusion | bytes 6422556 | tf_op jit(solution)/shard_map/dynamic_slice | solution.py:127
  23.8 33.6 %collective-permute-done = bf16[32,2,3584]{2,1,0:T(2,128)(2,1)S(1)} collective-permute-done((bf16[32,2,3584]{2,1,0:T(2,128)(2,1)}, bf16[32,2,3584]{2,1,0:T(2,128)(2,1)S(1)}, u32[]{:S(2)}, u32[]{:S(2)}) %collective-permute-start) | collective-permute-done | bytes 458784 | tf_op jit(solution)/shard_map/ppermute | solution.py:130
  57.3 6.6 %collective-permute-start.1 = (bf16[32,2,3584]{2,1,0:T(2,128)(2,1)}, bf16[32,2,3584]{2,1,0:T(2,128)(2,1)S(1)}, u32[]{:S(2)}, u32[]{:S(2)}) collective-permute-start(bf16[32,2,3584]{2,1,0:T(2,128)(2,1)} %get-tuple-element.75), channel_id=1, source_target_pairs={{0,2},{1,3},{2,4},{3,5},{4,6},{5,7},{6,0},{7,1},{8,10},{9,11},{10,... | collective-permute-start | bytes 1376264 | tf_op jit(solution)/shard_map/ppermute | solution.py:130
  65.1 8.1 %collective-permute-done.1 = bf16[32,2,3584]{2,1,0:T(2,128)(2,1)S(1)} collective-permute-done((bf16[32,2,3584]{2,1,0:T(2,128)(2,1)}, bf16[32,2,3584]{2,1,0:T(2,128)(2,1)S(1)}, u32[]{:S(2)}, u32[]{:S(2)}) %collective-permute-start.1) | collective-permute-done | bytes 458784 | tf_op jit(solution)/shard_map/ppermute | solution.py:130
  79.2 7.3 %collective-permute-done.5 = bf16[32,2,3584]{2,1,0:T(2,128)(2,1)S(1)} collective-permute-done((bf16[32,2,3584]{2,1,0:T(2,128)(2,1)S(1)}, bf16[32,2,3584]{2,1,0:T(2,128)(2,1)S(1)}, u32[]{:S(2)}, u32[]{:S(2)}) %collective-permute-start.5) | collective-permute-done | bytes 458784 | tf_op jit(solution)/shard_map/ppermute | solution.py:130
  88.7 11.6 %gather_fusion.1 = bf16[8,32,2,3584]{3,2,1,0:T(2,128)(2,1)} fusion(bf16[8,32,2,3584]{3,2,1,0:T(2,128)(2,1)} %bitcast_dynamic-update-slice_fusion, s32[1024]{0:T(1024)S(1)} %pad_clamp_fusion.2), kind=kCustom, calls=%fused_computation.1 | custom fusion | bytes 7340064 | tf_op jit(solution)/shard_map/jit(_take)/gather | solution.py:134
  100.3 9.2 %gather.20 = bf16[256,56,128]{2,1,0:T(8,128)(2,1)} reshape(bf16[8,32,2,3584]{3,2,1,0:T(2,128)(2,1)} %gather_fusion.1) | data formatting | bytes 7340032 | tf_op jit(solution)/shard_map/jit(_take)/gather | solution.py:134
  109.5 4.4 %fusion.12 = bf16[56,256,128]{2,1,0:T(8,128)(2,1)} fusion(bf16[256,56,128]{2,1,0:T(8,128)(2,1)} %gather.20, pred[256]{0:T(512)(128)(4,1)S(1)} %broadcast_in_dim.271), kind=kLoop, calls=%fused_computation.52 | loop fusion | flops 1835008 | bytes 7340288 | tf_op jit(solution)/shard_map/transpose | solution.py:147
  113.8 8.7 %gather_fusion.2 = bf16[128,256,128]{2,1,0:T(8,128)(2,1)} fusion(bf16[56,256,128]{2,1,0:T(8,128)(2,1)} %fusion.12, s32[1024]{0:T(1024)S(1)} %pad_clamp_fusion.1), kind=kCustom, calls=%fused_computation.2 | custom fusion | bytes 16777728 | tf_op jit(solution)/shard_map/jit(_take)/gather | solution.py:148
  122.5 6.4 %copy.123 = bf16[256,8192]{0,1:T(8,128)(2,1)} copy(bf16[256,8192]{1,0:T(8,128)(2,1)} %all-gather.2.cloned.1.call-done) | data formatting | bytes 8388608 | tf_op jit(solution)/shard_map/all_gather | solution.py:155
  128.9 6.4 %copy.124 = bf16[256,64,128]{2,0,1:T(8,128)(2,1)} copy(bf16[256,64,128]{0,2,1:T(8,128)(2,1)} %bitcast.248) | data formatting | bytes 8388608 | tf_op jit(solution)/shard_map/reshape | solution.py:158
  135.4 9.0 %gather_fusion = bf16[128,256,128]{2,1,0:T(8,128)(2,1)} fusion(bf16[64,256,128]{2,1,0:T(8,128)(2,1)} %bitcast.235, s32[1024]{0:T(1024)S(1)} %pad_clamp_fusion.3), kind=kCustom, calls=%fused_computation | custom fusion | bytes 16777728 | tf_op jit(solution)/shard_map/jit(_take)/gather | solution.py:160
  144.4 7.5 %broadcast_select_fusion = bf16[128,256,128]{2,1,0:T(8,128)(2,1)} fusion(bf16[128,256,128]{2,1,0:T(8,128)(2,1)} %gather_fusion, pred[128]{0:T(512)(128)(4,1)S(1)} %get-tuple-element.119), kind=kLoop, calls=%fused_computation.7 | loop fusion | flops 4194304 | bytes 16777344 | tf_op jit(solution)/shard_map/jit(_take)/select_n | solution.py:160
  151.9 11.7 %fusion = f32[128,128,128]{2,1,0:T(8,128)} fusion(bf16[128,256,128]{2,1,0:T(8,128)(2,1)} %broadcast_select_fusion, bf16[128,256,128]{2,1,0:T(8,128)(2,1)} %gather_fusion.2, pred[128]{0:T(512)(128)(4,1)S(1)} %get-tuple-element.118), kind=kOutput, calls=%fused_computation.4 | convolution fusion | flops 1077936128 | bytes 25165952 | tf_op jit(solution)/shard_map/kni,kno->kio/dot_general | solution.py:161
  163.6 14.0 %gather_fusion.3 = f32[192,128,128]{2,1,0:T(8,128)} fusion(f32[128,128,128]{2,1,0:T(8,128)} %fusion, s32[1024]{0:T(1024)S(1)} %pad_clamp_fusion), kind=kCustom, calls=%fused_computation.3 | custom fusion | bytes 25166592 | tf_op jit(solution)/shard_map/jit(_take)/gather | solution.py:48
  177.6 10.1 %broadcast_select_fusion.1 = f32[192,128,128]{2,1,0:T(8,128)} fusion(f32[192,128,128]{2,1,0:T(8,128)} %gather_fusion.3, pred[192]{0:T(512)(128)(4,1)S(1)} %compare_and_fusion.3), kind=kLoop, calls=%fused_computation.8 | loop fusion | flops 3145728 | bytes 25166016 | tf_op jit(solution)/shard_map/jit(_take)/select_n | solution.py:48
  187.7 8.8 %fusion.149 = (f32[96,128,128]{2,1,0:T(8,128)S(1)}, f32[96,128,128]{2,1,0:T(8,128)}) fusion(f32[192,128,128]{2,1,0:T(8,128)} %broadcast_select_fusion.1), kind=kLoop, calls=%fused_computation.262 | loop fusion | bytes 25165824 | tf_op jit(solution)/shard_map/slice | solution.py:50
  203.9 17.1 %collective-permute-done.16 = f32[24,64,128]{2,1,0:T(8,128)S(1)} collective-permute-done((f32[24,64,128]{2,1,0:T(8,128)}, f32[24,64,128]{2,1,0:T(8,128)S(1)}, u32[]{:S(2)}, u32[]{:S(2)}) %collective-permute-start.16) | collective-permute-done | bytes 786464 | tf_op jit(solution)/shard_map/ppermute | solution.py:94
  227.4 6.0 %collective-permute-start.10 = (f32[12,64,128]{2,1,0:T(8,128)S(1)}, f32[12,64,128]{2,1,0:T(8,128)S(1)}, u32[]{:S(2)}, u32[]{:S(2)}) collective-permute-start(f32[12,64,128]{2,1,0:T(8,128)S(1)} %get-tuple-element.69), channel_id=1, source_target_pairs={{0,56},{8,0},{16,8},{24,16},{32,24},{40,32},{48,40},{56,48},{64,12... | collective-permute-start | bytes 1179656 | tf_op jit(solution)/shard_map/ppermute | solution.py:94
  262.2 6.1 %fusion.13 = f32[128,64,128]{2,1,0:T(8,128)} fusion(bf16[128,128,128]{2,1,0:T(8,128)(2,1)} %param.9, bf16[128,256,128]{2,1,0:T(8,128)(2,1)} %broadcast_select_fusion), kind=kOutput, calls=%fused_computation.53 | convolution fusion | flops 268435456 | bytes 10485760 | tf_op jit(solution)/shard_map/kni,kio->kno/dot_general | solution.py:172
  290.5 5.0 %fusion.39 = bf16[64,56,128]{2,1,0:T(8,128)(2,1)} fusion(f32[128,64,128]{2,1,0:T(8,128)S(1)} %fusion.17, s32[128]{0:T(128)S(1)} %copy-done.6, pred[128]{0:T(512)(128)(4,1)S(1)} %iota_compare_fusion.4), kind=kOutput, calls=%fused_computation.83 | convolution fusion | flops 705116160 | bytes 5112448 | tf_op jit(solution)/shard_map/kc,kno->cno/dot_general | solution.py:173
  318.6 5.0 %fusion.36 = bf16[64,56,128]{2,1,0:T(8,128)(2,1)} fusion(f32[128,64,128]{2,1,0:T(8,128)S(1)} %fusion.15, s32[128]{0:T(128)S(1)} %copy-done.6, pred[128]{0:T(512)(128)(4,1)S(1)} %iota_compare_fusion.4), kind=kOutput, calls=%fused_computation.82 | convolution fusion | flops 705116160 | bytes 5112448 | tf_op jit(solution)/shard_map/kc,kno->cno/dot_general | solution.py:173
  349.2 5.0 %fusion.33 = bf16[64,56,128]{2,1,0:T(8,128)(2,1)} fusion(f32[128,64,128]{2,1,0:T(8,128)S(1)} %copy-done.3, s32[128]{0:T(128)S(1)} %copy-done.6, pred[128]{0:T(512)(128)(4,1)S(1)} %iota_compare_fusion.4), kind=kOutput, calls=%fused_computation.81 | convolution fusion | flops 705116160 | bytes 5112448 | tf_op jit(solution)/shard_map/kc,kno->cno/dot_general | solution.py:173
  359.2 7.4 %pad_maximum_fusion = bf16[256,2,3584]{2,1,0:T(2,128)(2,1)} fusion(bf16[64,2,3584]{2,1,0:T(2,128)(2,1)} %reshape.233, bf16[64,2,3584]{2,1,0:T(2,128)(2,1)} %reshape.232, bf16[64,2,3584]{2,1,0:T(2,128)(2,1)} %reshape.231, bf16[64,2,3584]{2,1,0:T(2,128)(2,1)S(1)} %reshape.230), kind=kLoop, calls=%fused_computation.50 | loop fusion | flops 5505024 | bytes 7340032 | tf_op jit(solution)/shard_map/concatenate | solution.py:183
  (180 shorter events, 149.4 us)
Async XLA Ops:
  7.2 115.4 %all-gather.2.cloned.1.call-start = ((), (), s32[]{:S(2)}) async-start(), calls=%async_computation | async-start | bytes 4718592 | tf_op jit(solution)/shard_map/all_gather | solution.py:155
  12.7 74.9 %collective-permute-start.6 = (bf16[32,2,3584]{2,1,0:T(2,128)(2,1)S(1)}, bf16[32,2,3584]{2,1,0:T(2,128)(2,1)S(1)}, u32[]{:S(2)}, u32[]{:S(2)}) collective-permute-start(bf16[32,2,3584]{2,1,0:T(2,128)(2,1)S(1)} %get-tuple-element.71), channel_id=1, source_target_pairs={{0,7},{1,0},{2,1},{3,2},{4,3},{5,4},{6,5},{7,6},{8,15},{9,8},{10,9... | collective-permute-start | bytes 1376264 | tf_op jit(solution)/shard_map/ppermute | solution.py:130
  15.1 63.0 %collective-permute-start.4 = (bf16[32,2,3584]{2,1,0:T(2,128)(2,1)}, bf16[32,2,3584]{2,1,0:T(2,128)(2,1)S(1)}, u32[]{:S(2)}, u32[]{:S(2)}) collective-permute-start(bf16[32,2,3584]{2,1,0:T(2,128)(2,1)} %get-tuple-element.72), channel_id=1, source_target_pairs={{0,5},{1,6},{2,7},{3,0},{4,1},{5,2},{6,3},{7,4},{8,13},{9,14},{10,... | collective-permute-start | bytes 1376264 | tf_op jit(solution)/shard_map/ppermute | solution.py:130
  16.0 61.0 %collective-permute-start.3 = (bf16[32,2,3584]{2,1,0:T(2,128)(2,1)}, bf16[32,2,3584]{2,1,0:T(2,128)(2,1)S(1)}, u32[]{:S(2)}, u32[]{:S(2)}) collective-permute-start(bf16[32,2,3584]{2,1,0:T(2,128)(2,1)} %get-tuple-element.73), channel_id=1, source_target_pairs={{0,4},{1,5},{2,6},{3,7},{4,0},{5,1},{6,2},{7,3},{8,12},{9,13},{10,... | collective-permute-start | bytes 1376264 | tf_op jit(solution)/shard_map/ppermute | solution.py:130
  16.3 59.6 %collective-permute-start.2 = (bf16[32,2,3584]{2,1,0:T(2,128)(2,1)}, bf16[32,2,3584]{2,1,0:T(2,128)(2,1)S(1)}, u32[]{:S(2)}, u32[]{:S(2)}) collective-permute-start(bf16[32,2,3584]{2,1,0:T(2,128)(2,1)} %get-tuple-element.74), channel_id=1, source_target_pairs={{0,3},{1,4},{2,5},{3,6},{4,7},{5,0},{6,1},{7,2},{8,11},{9,12},{10,... | collective-permute-start | bytes 1376264 | tf_op jit(solution)/shard_map/ppermute | solution.py:130
  16.9 40.5 %collective-permute-start = (bf16[32,2,3584]{2,1,0:T(2,128)(2,1)}, bf16[32,2,3584]{2,1,0:T(2,128)(2,1)S(1)}, u32[]{:S(2)}, u32[]{:S(2)}) collective-permute-start(bf16[32,2,3584]{2,1,0:T(2,128)(2,1)} %get-tuple-element.76), channel_id=1, source_target_pairs={{0,1},{1,2},{2,3},{3,4},{4,5},{5,6},{6,7},{7,0},{8,9},{9,10},{10,1... | collective-permute-start | bytes 1376264 | tf_op jit(solution)/shard_map/ppermute | solution.py:130
  57.3 15.8 %collective-permute-start.1 = (bf16[32,2,3584]{2,1,0:T(2,128)(2,1)}, bf16[32,2,3584]{2,1,0:T(2,128)(2,1)S(1)}, u32[]{:S(2)}, u32[]{:S(2)}) collective-permute-start(bf16[32,2,3584]{2,1,0:T(2,128)(2,1)} %get-tuple-element.75), channel_id=1, source_target_pairs={{0,2},{1,3},{2,4},{3,5},{4,6},{5,7},{6,0},{7,1},{8,10},{9,11},{10,... | collective-permute-start | bytes 1376264 | tf_op jit(solution)/shard_map/ppermute | solution.py:130
  73.2 13.3 %collective-permute-start.5 = (bf16[32,2,3584]{2,1,0:T(2,128)(2,1)S(1)}, bf16[32,2,3584]{2,1,0:T(2,128)(2,1)S(1)}, u32[]{:S(2)}, u32[]{:S(2)}) collective-permute-start(bf16[32,2,3584]{2,1,0:T(2,128)(2,1)S(1)} %get-tuple-element.77), channel_id=1, source_target_pairs={{0,6},{1,7},{2,0},{3,1},{4,2},{5,3},{6,4},{7,5},{8,14},{9,15},{10,... | collective-permute-start | bytes 1376264 | tf_op jit(solution)/shard_map/ppermute | solution.py:130
  200.4 20.6 %collective-permute-start.16 = (f32[24,64,128]{2,1,0:T(8,128)}, f32[24,64,128]{2,1,0:T(8,128)S(1)}, u32[]{:S(2)}, u32[]{:S(2)}) collective-permute-start(f32[24,64,128]{2,1,0:T(8,128)} %get-tuple-element.63), channel_id=1, source_target_pairs={{0,192},{8,200},{16,208},{24,216},{32,224},{40,232},{48,240},{56,2... | collective-permute-start | bytes 2359304 | tf_op jit(solution)/shard_map/ppermute | solution.py:94
  201.2 19.8 %collective-permute-start.13 = (f32[24,64,128]{2,1,0:T(8,128)}, f32[24,64,128]{2,1,0:T(8,128)S(1)}, u32[]{:S(2)}, u32[]{:S(2)}) collective-permute-start(f32[24,64,128]{2,1,0:T(8,128)} %get-tuple-element.64), channel_id=1, source_target_pairs={{0,64},{8,72},{16,80},{24,88},{32,96},{40,104},{48,112},{56,120},{... | collective-permute-start | bytes 2359304 | tf_op jit(solution)/shard_map/ppermute | solution.py:93
  222.7 25.3 %collective-permute-start.17 = (f32[24,64,128]{2,1,0:T(8,128)S(1)}, f32[24,64,128]{2,1,0:T(8,128)S(1)}, u32[]{:S(2)}, u32[]{:S(2)}) collective-permute-start(f32[24,64,128]{2,1,0:T(8,128)S(1)} %get-tuple-element.61), channel_id=1, source_target_pairs={{0,192},{8,200},{16,208},{24,216},{32,224},{40,232},{48,240},{56,2... | collective-permute-start | bytes 2359304 | tf_op jit(solution)/shard_map/ppermute | solution.py:94
  222.7 25.2 %collective-permute-start.14 = (f32[24,64,128]{2,1,0:T(8,128)S(1)}, f32[24,64,128]{2,1,0:T(8,128)S(1)}, u32[]{:S(2)}, u32[]{:S(2)}) collective-permute-start(f32[24,64,128]{2,1,0:T(8,128)S(1)} %get-tuple-element.62), channel_id=1, source_target_pairs={{0,64},{8,72},{16,80},{24,88},{32,96},{40,104},{48,112},{56,120},{... | collective-permute-start | bytes 2359304 | tf_op jit(solution)/shard_map/ppermute | solution.py:93
  227.4 12.9 %collective-permute-start.10 = (f32[12,64,128]{2,1,0:T(8,128)S(1)}, f32[12,64,128]{2,1,0:T(8,128)S(1)}, u32[]{:S(2)}, u32[]{:S(2)}) collective-permute-start(f32[12,64,128]{2,1,0:T(8,128)S(1)} %get-tuple-element.69), channel_id=1, source_target_pairs={{0,56},{8,0},{16,8},{24,16},{32,24},{40,32},{48,40},{56,48},{64,12... | collective-permute-start | bytes 1179656 | tf_op jit(solution)/shard_map/ppermute | solution.py:94
  245.9 12.4 %collective-permute-start.11 = (f32[12,64,128]{2,1,0:T(8,128)}, f32[12,64,128]{2,1,0:T(8,128)S(1)}, u32[]{:S(2)}, u32[]{:S(2)}) collective-permute-start(f32[12,64,128]{2,1,0:T(8,128)} %get-tuple-element.67), channel_id=1, source_target_pairs={{0,56},{8,0},{16,8},{24,16},{32,24},{40,32},{48,40},{56,48},{64,12... | collective-permute-start | bytes 1179656 | tf_op jit(solution)/shard_map/ppermute | solution.py:94
  246.2 12.2 %collective-permute-start.8 = (f32[12,64,128]{2,1,0:T(8,128)}, f32[12,64,128]{2,1,0:T(8,128)}, u32[]{:S(2)}, u32[]{:S(2)}) collective-permute-start(f32[12,64,128]{2,1,0:T(8,128)} %get-tuple-element.68), channel_id=1, source_target_pairs={{0,8},{8,16},{16,24},{24,32},{32,40},{40,48},{48,56},{56,0},{64,72... | collective-permute-start | bytes 1179656 | tf_op jit(solution)/shard_map/ppermute | solution.py:93
  250.8 19.9 %collective-permute-start.18 = (f32[24,64,128]{2,1,0:T(8,128)}, f32[24,64,128]{2,1,0:T(8,128)S(1)}, u32[]{:S(2)}, u32[]{:S(2)}) collective-permute-start(f32[24,64,128]{2,1,0:T(8,128)} %get-tuple-element.59), channel_id=1, source_target_pairs={{0,192},{8,200},{16,208},{24,216},{32,224},{40,232},{48,240},{56,2... | collective-permute-start | bytes 2359304 | tf_op jit(solution)/shard_map/ppermute | solution.py:94
  250.8 19.9 %collective-permute-start.15 = (f32[24,64,128]{2,1,0:T(8,128)}, f32[24,64,128]{2,1,0:T(8,128)}, u32[]{:S(2)}, u32[]{:S(2)}) collective-permute-start(f32[24,64,128]{2,1,0:T(8,128)} %get-tuple-element.60), channel_id=1, source_target_pairs={{0,64},{8,72},{16,80},{24,88},{32,96},{40,104},{48,112},{56,120},{... | collective-permute-start | bytes 2359304 | tf_op jit(solution)/shard_map/ppermute | solution.py:93
  280.3 18.2 %collective-permute-start.26 = (f32[3,64,128]{2,1,0:T(8,128)}, f32[3,64,128]{2,1,0:T(8,128)S(1)}, u32[]{:S(2)}, u32[]{:S(2)}) collective-permute-start(f32[3,64,128]{2,1,0:T(8,128)} %get-tuple-element.84), channel_id=1, source_target_pairs={{0,56},{8,0},{16,8},{24,16},{32,24},{40,32},{48,40},{56,48},{64,12... | collective-permute-start | bytes 294920 | tf_op jit(solution)/shard_map/ppermute | solution.py:94
  286.9 11.5 %collective-permute-start.22 = (f32[12,64,128]{2,1,0:T(8,128)}, f32[12,64,128]{2,1,0:T(8,128)S(1)}, u32[]{:S(2)}, u32[]{:S(2)}) collective-permute-start(f32[12,64,128]{2,1,0:T(8,128)} %get-tuple-element.55), channel_id=1, source_target_pairs={{0,56},{8,0},{16,8},{24,16},{32,24},{40,32},{48,40},{56,48},{64,12... | collective-permute-start | bytes 1179656 | tf_op jit(solution)/shard_map/ppermute | solution.py:94
  308.6 18.1 %collective-permute-start.34 = (f32[3,64,128]{2,1,0:T(8,128)S(1)}, f32[3,64,128]{2,1,0:T(8,128)}, u32[]{:S(2)}, u32[]{:S(2)}) collective-permute-start(f32[3,64,128]{2,1,0:T(8,128)S(1)} %get-tuple-element.82), channel_id=1, source_target_pairs={{0,56},{8,0},{16,8},{24,16},{32,24},{40,32},{48,40},{56,48},{64,12... | collective-permute-start | bytes 294920 | tf_op jit(solution)/shard_map/ppermute | solution.py:94
  333.6 23.6 %collective-permute-start.42 = (f32[3,64,128]{2,1,0:T(8,128)S(1)}, f32[3,64,128]{2,1,0:T(8,128)S(1)}, u32[]{:S(2)}, u32[]{:S(2)}) collective-permute-start(f32[3,64,128]{2,1,0:T(8,128)S(1)} %get-tuple-element.80), channel_id=1, source_target_pairs={{0,56},{8,0},{16,8},{24,16},{32,24},{40,32},{48,40},{56,48},{64,12... | collective-permute-start | bytes 294920 | tf_op jit(solution)/shard_map/ppermute | solution.py:94
  339.3 17.9 %collective-permute-start.38 = (f32[3,64,128]{2,1,0:T(8,128)}, f32[3,64,128]{2,1,0:T(8,128)}, u32[]{:S(2)}, u32[]{:S(2)}) collective-permute-start(f32[3,64,128]{2,1,0:T(8,128)} %get-tuple-element.88), channel_id=1, source_target_pairs={{0,192},{8,200},{16,208},{24,216},{32,224},{40,232},{48,240},{56,2... | collective-permute-start | bytes 294920 | tf_op jit(solution)/shard_map/ppermute | solution.py:94
  343.4 13.8 %collective-permute-start.40 = (f32[3,64,128]{2,1,0:T(8,128)}, f32[3,64,128]{2,1,0:T(8,128)}, u32[]{:S(2)}, u32[]{:S(2)}) collective-permute-start(f32[3,64,128]{2,1,0:T(8,128)} %fusion.129), channel_id=1, source_target_pairs={{0,8},{8,16},{16,24},{24,32},{32,40},{40,48},{48,56},{56,0},{64,72... | collective-permute-start | bytes 294920 | tf_op jit(solution)/shard_map/ppermute | solution.py:93
  345.4 11.8 %collective-permute-start.36 = (f32[3,64,128]{2,1,0:T(8,128)}, f32[3,64,128]{2,1,0:T(8,128)}, u32[]{:S(2)}, u32[]{:S(2)}) collective-permute-start(f32[3,64,128]{2,1,0:T(8,128)} %fusion.105), channel_id=1, source_target_pairs={{0,64},{8,72},{16,80},{24,88},{32,96},{40,104},{48,112},{56,120},{... | collective-permute-start | bytes 294920 | tf_op jit(solution)/shard_map/ppermute | solution.py:93
  (33 other events, 304.0 us)
Sparse Core Ops, SparseCore 0:
  9.9 56.1 all-gather.1
